TPU v7x, 256 devices: a whole 4x4x8 slice. The times are simulated.
256 devices in a mesh: req: 32 (over z, x_lo, core), tp: 8 (over x_hi, y).
Axes of the slice: x: 4 (x_hi: 2, x_lo: 2; x = x_hi * 2 + x_lo), y: 4, z: 8, core: 2. Of those that a mesh axis runs over, the one named last changes fastest.
Arguments:
- queries: bfloat16 [12288, 8192], P('req', 'tp'), may hold values from -40 to 40
- suffix_kv: bfloat16 [2, 12288, 1024], P(None, 'req', 'tp'), may hold values from -4 to 4
- prefix_kv: bfloat16 [2, 32, 256, 1024], P(None, 'req', 'tp'), may hold values from -4 to 4
- suffix_length: int32 [31], replicated, may hold values from 16 to 384, as said below
- request_group: int32 [31], replicated, may hold values from 0 to 3
- request_order: int32 [31], replicated, may hold values from 0 to 30, each once
- owner_map: int32 [32], replicated, may hold values from 0 to 31, each once
Outputs:
- attention: bfloat16 [12288, 8192], P('req', 'tp')
Inputs may be any that keep to these rules, and one draw needn't show every extreme that they name: `suffix_length`: every suffix has 16 to 384 tokens; in every draw one suffix has exactly 384 tokens and one exactly 16.
All inputs are finite; a program needn't handle non-finite values.
Results may differ from a plain program's by a relative error of at most 0.007.
Values may be sent and summed in bfloat16 or wider, within the bound.
No kernel may reach another device: no remote copies, remote signals or barrier semaphores. Data moves between devices by JAX's collectives and lax.ppermute only.
A program may use at most 128 MiB of HBM per device.

v0:
```python
import math
import jax
import jax.numpy as jnp
from jax import lax
from jax.sharding import PartitionSpec as P

QH = 64
KVH = 8
HD = 128
GROUPS = 4
masked_score = -1e30


def from_behind(block, axis, distance):
    devices = range(lax.axis_size(axis))
    route = [(i - distance, i) for i in devices if i - distance in devices]
    return lax.ppermute(block, axis, route)


def pack_index(slot_ids, starts, stops):
    inside = (starts[None, :] <= slot_ids[:, None]) & (slot_ids[:, None] < stops[None, :])
    request_ids = jnp.arange(starts.shape[0], dtype=jnp.int32)
    found = jnp.sum(jnp.where(inside, request_ids[None, :], 0), axis=1)
    missing = jnp.where(jnp.any(inside, axis=1), 0, starts.shape[0]).astype(jnp.int32)
    return found + missing


def pick_rows(lookup, selector, extent):
    matches = selector[:, None] == jnp.arange(extent, dtype=jnp.int32)[None, :]
    return jnp.sum(jnp.where(matches, lookup[None, :], 0), axis=1)


def per_device(
    queries, suffix_kv, prefix_kv, suffix_length, request_group, request_order, owner_map
):
    tok_rows = queries.shape[0]
    head_cols = suffix_kv.shape[2]
    kv_heads = head_cols // HD
    per_kv = QH // KVH
    stored_count = owner_map.shape[0]
    per_group = stored_count // GROUPS
    requests = suffix_length.shape[0]
    score_scale = 1.0 / math.sqrt(HD)
    packed_length = pick_rows(suffix_length, request_order, requests)
    packed_group = pick_rows(request_group, request_order, requests)
    starts = (jnp.arange(requests, dtype=jnp.int32) + 1) * tok_rows - packed_length // 2
    stops = starts + packed_length
    device = lax.axis_index("req")
    slot_ids = device * tok_rows + jnp.arange(tok_rows, dtype=jnp.int32)
    own_pack = pack_index(slot_ids, starts, stops)
    is_live = own_pack < requests
    slot_group = pick_rows(packed_group, own_pack, requests)
    block_ids = jnp.arange(stored_count, dtype=jnp.int32)
    stored_group = jnp.sum(
        jnp.where(owner_map[None, :] == block_ids[:, None], (block_ids // per_group)[None, :], 0),
        axis=1,
    )
    query_heads = queries.reshape(tok_rows, kv_heads, per_kv, HD)

    def absorb(carried, key_rows, value_rows, allowed):
        running_max, running_sum, running_acc = carried
        scores = (
            jnp.einsum("tjqd,kjd->jtqk", query_heads, key_rows, preferred_element_type=jnp.float32)
            * score_scale
        )
        visible = allowed[None, :, None, :]
        scores = jnp.where(visible, scores, masked_score)
        new_max = jnp.maximum(running_max, jnp.max(scores, axis=-1))
        weights = jnp.where(visible, jnp.exp(scores - new_max[..., None]), 0.0)
        shrink = jnp.exp(running_max - new_max)
        new_sum = running_sum * shrink + jnp.sum(weights, axis=-1)
        product = jnp.einsum(
            "jtqk,kjd->jtqd",
            weights.astype(jnp.bfloat16),
            value_rows,
            preferred_element_type=jnp.float32,
        )
        return (new_max, new_sum, running_acc * shrink[..., None] + product)

    earlier = from_behind(suffix_kv, "req", 1)
    nearby = jnp.concatenate([earlier, suffix_kv], axis=1)
    near_slots = device * tok_rows - tok_rows + jnp.arange(2 * tok_rows, dtype=jnp.int32)
    near_pack = pack_index(near_slots, starts, stops)
    near_allowed = (
        (near_pack[None, :] == own_pack[:, None])
        & (near_slots[None, :] <= slot_ids[:, None])
        & (near_slots[None, :] >= 0)
        & is_live[:, None]
    )
    initial = (
        jnp.full((kv_heads, tok_rows, per_kv), masked_score, jnp.float32),
        jnp.zeros((kv_heads, tok_rows, per_kv), jnp.float32),
        jnp.zeros((kv_heads, tok_rows, per_kv, HD), jnp.float32),
    )
    carried = absorb(
        initial,
        nearby[0].reshape(2 * tok_rows, kv_heads, HD),
        nearby[1].reshape(2 * tok_rows, kv_heads, HD),
        near_allowed,
    )
    stored = lax.all_gather(prefix_kv, "req", axis=1, tiled=True)
    relaid = lax.all_to_all(stored, "tp", split_axis=3, concat_axis=2, tiled=True)
    status = carried
    extent = relaid.shape[1]
    block_rows = relaid.shape[2]
    stride = math.gcd(extent, max(1, 512 // block_rows))
    passes = extent // stride
    key_rows = relaid[0].reshape(passes, stride * block_rows, kv_heads, HD)
    value_rows = relaid[1].reshape(passes, stride * block_rows, kv_heads, HD)
    key_groups = jnp.repeat(stored_group, block_rows).reshape(passes, stride * block_rows)

    def visit_block(inner, inputs):
        keys_here, values_here, groups_here = inputs
        allowed = (groups_here[None, :] == slot_group[:, None]) & is_live[:, None]
        inner = absorb(inner, keys_here, values_here, allowed)
        return (inner, None)

    status, unused = lax.scan(visit_block, status, (key_rows, value_rows, key_groups))
    carried = status
    running_max, running_sum, running_acc = carried
    divisor = jnp.where(is_live[None, :, None], running_sum, 1.0)
    result = jnp.where(is_live[None, :, None, None], running_acc / divisor[..., None], 0.0)
    return (
        jnp.transpose(result, (1, 0, 2, 3))
        .reshape(tok_rows, kv_heads * per_kv * HD)
        .astype(jnp.bfloat16)
    )


def solution(mesh):
    in_specs = (
        P("req", "tp"),
        P(None, "req", "tp"),
        P(None, "req", "tp", None),
        P(),
        P(),
        P(),
        P(),
    )
    out_specs = P("req", "tp")
    return jax.shard_map(
        per_device, mesh=mesh, in_specs=in_specs, out_specs=out_specs, check_vma=False
    )
```

profile of v0, /device:TPU:1, one launch (start us, length us, event | category | flops | bytes accessed | tf_op | source)
XLA Modules:
  0.0 346.6 jit_solution(16441505130025673132)
XLA Ops:
  7.3 4.5 %collective-permute-start = (bf16[2,384,128]{2,1,0:T(8,128)(2,1)}, bf16[2,384,128]{2,1,0:T(8,128)(2,1)S(1)}, u32[]{:S(2)}, u32[]{:S(2)}) collective-permute-start(bf16[2,384,128]{2,1,0:T(8,128)(2,1)} %param.10), channel_id=1, source_target_pairs={{0,8},{8,16},{16,24},{24,32},{32,40},{40,48},{48,56},{56,64},{64,7... | collective-permute-start | bytes 589832 | tf_op jit(solution)/shard_map/ppermute | solution.py:17
  11.8 1.5 copy.45
  15.8 64.1 %all-gather.2.cloned.1.call-done = bf16[2,32,32,1024]{3,2,0,1:T(8,128)(2,1)} async-done(((bf16[2,1,32,1024]{3,2,0,1:T(8,128)(2,1)}), bf16[2,32,32,1024]{3,2,0,1:T(8,128)(2,1)}) %all-gather.2.cloned.1.call-update) | async-done | bytes 4194320 | tf_op jit(solution)/shard_map/all_gather | solution.py:101
  79.9 23.2 %copy.43 = bf16[2,32,32,1024]{2,1,0,3:T(8,128)(2,1)} copy(bf16[2,32,32,1024]{3,2,0,1:T(8,128)(2,1)} %all-gather.2.cloned.1.call-done) | data formatting | bytes 8388608 | tf_op jit(solution)/shard_map/all_gather | solution.py:101
  103.1 18.7 %reshape.344 = bf16[8,2,131072]{2,1,0:T(2,128)(2,1)} reshape(bf16[1024,2,32,32]{3,2,1,0:T(8,128)(2,1)} %bitcast.120) | data formatting | bytes 8388608
  121.8 6.3 %all-to-all-start = ((bf16[8,2,131072]{2,1,0:T(2,128)(2,1)}), bf16[8,2,131072]{2,1,0:T(2,128)(2,1)}, u32[]{:S(2)}, u32[]{:S(2)}) async-start(bf16[8,2,131072]{2,1,0:T(2,128)(2,1)} %reshape.344), calls=%async_computation | async-start | bytes 8388608 | tf_op jit(solution)/shard_map/all_to_all | solution.py:102
  129.1 1.6 fusion.20
  130.8 2.2 fusion.22
  133.1 4.0 %add_bitcast_fusion = f32[1,384,8,128]{3,1,2,0:T(8,128)} fusion(f32[768,384,8]{1,0,2:T(8,128)S(1)} %get-tuple-element.136, f32[384,8]{0,1:T(8,128)S(1)} %get-tuple-element.134, pred[384,768]{0,1:T(8,128)(4,1)S(1)} %and_and_fusion, f32[384,8]{0,1:T(8,128)S(1)} %get-tuple-element.132, bf16[2,768,128]{2,1,0:T(8,128)(2,1)S(1)} %constant_dynamic-update-slice_fusion), kind=kOutput, calls=%fused_computation.33 | convolution fusion | flops 616169472 | bytes 11526144 | tf_op jit(solution)/shard_map/jtqk,kjd->jtqd/dot_general | solution.py:72
  137.1 39.8 %all-to-all-done = bf16[8,2,131072]{2,1,0:T(2,128)(2,1)} async-done(((bf16[8,2,131072]{2,1,0:T(2,128)(2,1)}), bf16[8,2,131072]{2,1,0:T(2,128)(2,1)}, u32[]{:S(2)}, u32[]{:S(2)}) %all-to-all-start) | async-done | bytes 4194336 | tf_op jit(solution)/shard_map/all_to_all | solution.py:102
  176.8 12.4 %reshape.345 = bf16[1024,2,32,32]{3,2,1,0:T(8,128)(2,1)} reshape(bf16[8,2,131072]{2,1,0:T(2,128)(2,1)} %all-to-all-done) | data formatting | bytes 8388608
  189.3 12.6 %fusion.40 = (bf16[1,32,8,32,128]{3,1,0,4,2:T(8,128)(2,1)}, bf16[1,32,8,32,128]{3,1,0,4,2:T(8,128)(2,1)}) fusion(bf16[2,32,8,32,128]{3,1,0,4,2:T(8,128)(2,1)} %bitcast.121), kind=kLoop, calls=%fused_computation.80 | loop fusion | bytes 8388608 | tf_op jit(solution)/shard_map/slice | solution.py:109
  201.8 8.5 %copy.44 = bf16[1,32,8,32,128]{4,3,2,1,0:T(8,128)(2,1)S(1)} copy(bf16[1,32,8,32,128]{3,1,0,4,2:T(8,128)(2,1)} %get-tuple-element.131) | data formatting | bytes 4194304 | tf_op jit(solution)/shard_map/slice | solution.py:108
  210.3 9.3 %copy.46 = bf16[1,32,8,32,128]{4,3,2,1,0:T(8,128)(2,1)} copy(bf16[1,32,8,32,128]{3,1,0,4,2:T(8,128)(2,1)} %get-tuple-element.130) | data formatting | bytes 4194304 | tf_op jit(solution)/shard_map/slice | solution.py:109
  219.7 116.5 %while.14 = (s32[]{:T(128)}, f32[1,384,8]{1,2,0:T(8,128)S(1)}, f32[1,384,8]{1,2,0:T(8,128)S(1)}, f32[1,384,8,128]{3,1,2,0:T(8,128)}, s32[16,512]{1,0:T(8,128)S(1...) while((s32[]{:T(128)}, f32[1,384,8]{1,2,0:T(8,128)S(1)}, ...), condition=%wide.region_13.14_spmd, body=%wide.region_10.13_spmd.sunk | while | flops 826942464 | bytes 24060404 | solution.py:118
  221.0 4.4 %bitcast_add_fusion.6 = f32[1,384,8,128]{3,1,2,0:T(8,128)} fusion(f32[1,384,8,128]{3,1,2,0:T(8,128)} %get-tuple-element.220, f32[512,384,8]{1,0,2:T(8,128)S(1)} %get-tuple-element.204, f32[384,8]{0,1:T(8,128)S(1)} %bitcast.122, pred[384,512]{0,1:T(8,128)(4,1)S(1)} %compare_and_fusion.4, f32[384,8]{0,1:T(8,128)S(1)} %get-tuple-element.205, ...), kind=kOutput, calls=%fused_computation.7.clone.1 | convolution fusion | flops 411303936 | bytes 9789952 | tf_op jit(solution)/shard_map/while/body/eval_jaxpr/jtqk,kjd->jtqd/dot_general | solution.py:72
  225.4 1.5 fusion.51
  228.3 4.4 %bitcast_add_fusion.6 = f32[1,384,8,128]{3,1,2,0:T(8,128)} fusion(f32[1,384,8,128]{3,1,2,0:T(8,128)} %get-tuple-element.220, f32[512,384,8]{1,0,2:T(8,128)S(1)} %get-tuple-element.204, f32[384,8]{0,1:T(8,128)S(1)} %bitcast.122, pred[384,512]{0,1:T(8,128)(4,1)S(1)} %compare_and_fusion.4, f32[384,8]{0,1:T(8,128)S(1)} %get-tuple-element.205, ...), kind=kOutput, calls=%fused_computation.7.clone.1 | convolution fusion | flops 411303936 | bytes 9789952 | tf_op jit(solution)/shard_map/while/body/eval_jaxpr/jtqk,kjd->jtqd/dot_general | solution.py:72
  232.7 1.5 fusion.51
  235.6 4.4 %bitcast_add_fusion.6 = f32[1,384,8,128]{3,1,2,0:T(8,128)} fusion(f32[1,384,8,128]{3,1,2,0:T(8,128)} %get-tuple-element.220, f32[512,384,8]{1,0,2:T(8,128)S(1)} %get-tuple-element.204, f32[384,8]{0,1:T(8,128)S(1)} %bitcast.122, pred[384,512]{0,1:T(8,128)(4,1)S(1)} %compare_and_fusion.4, f32[384,8]{0,1:T(8,128)S(1)} %get-tuple-element.205, ...), kind=kOutput, calls=%fused_computation.7.clone.1 | convolution fusion | flops 411303936 | bytes 9789952 | tf_op jit(solution)/shard_map/while/body/eval_jaxpr/jtqk,kjd->jtqd/dot_general | solution.py:72
  239.9 1.5 fusion.51
  242.9 4.4 %bitcast_add_fusion.6 = f32[1,384,8,128]{3,1,2,0:T(8,128)} fusion(f32[1,384,8,128]{3,1,2,0:T(8,128)} %get-tuple-element.220, f32[512,384,8]{1,0,2:T(8,128)S(1)} %get-tuple-element.204, f32[384,8]{0,1:T(8,128)S(1)} %bitcast.122, pred[384,512]{0,1:T(8,128)(4,1)S(1)} %compare_and_fusion.4, f32[384,8]{0,1:T(8,128)S(1)} %get-tuple-element.205, ...), kind=kOutput, calls=%fused_computation.7.clone.1 | convolution fusion | flops 411303936 | bytes 9789952 | tf_op jit(solution)/shard_map/while/body/eval_jaxpr/jtqk,kjd->jtqd/dot_general | solution.py:72
  247.2 1.5 fusion.51
  250.2 4.4 %bitcast_add_fusion.6 = f32[1,384,8,128]{3,1,2,0:T(8,128)} fusion(f32[1,384,8,128]{3,1,2,0:T(8,128)} %get-tuple-element.220, f32[512,384,8]{1,0,2:T(8,128)S(1)} %get-tuple-element.204, f32[384,8]{0,1:T(8,128)S(1)} %bitcast.122, pred[384,512]{0,1:T(8,128)(4,1)S(1)} %compare_and_fusion.4, f32[384,8]{0,1:T(8,128)S(1)} %get-tuple-element.205, ...), kind=kOutput, calls=%fused_computation.7.clone.1 | convolution fusion | flops 411303936 | bytes 9789952 | tf_op jit(solution)/shard_map/while/body/eval_jaxpr/jtqk,kjd->jtqd/dot_general | solution.py:72
  254.5 1.5 fusion.51
  257.4 4.4 %bitcast_add_fusion.6 = f32[1,384,8,128]{3,1,2,0:T(8,128)} fusion(f32[1,384,8,128]{3,1,2,0:T(8,128)} %get-tuple-element.220, f32[512,384,8]{1,0,2:T(8,128)S(1)} %get-tuple-element.204, f32[384,8]{0,1:T(8,128)S(1)} %bitcast.122, pred[384,512]{0,1:T(8,128)(4,1)S(1)} %compare_and_fusion.4, f32[384,8]{0,1:T(8,128)S(1)} %get-tuple-element.205, ...), kind=kOutput, calls=%fused_computation.7.clone.1 | convolution fusion | flops 411303936 | bytes 9789952 | tf_op jit(solution)/shard_map/while/body/eval_jaxpr/jtqk,kjd->jtqd/dot_general | solution.py:72
  261.8 1.5 fusion.51
  264.7 4.4 %bitcast_add_fusion.6 = f32[1,384,8,128]{3,1,2,0:T(8,128)} fusion(f32[1,384,8,128]{3,1,2,0:T(8,128)} %get-tuple-element.220, f32[512,384,8]{1,0,2:T(8,128)S(1)} %get-tuple-element.204, f32[384,8]{0,1:T(8,128)S(1)} %bitcast.122, pred[384,512]{0,1:T(8,128)(4,1)S(1)} %compare_and_fusion.4, f32[384,8]{0,1:T(8,128)S(1)} %get-tuple-element.205, ...), kind=kOutput, calls=%fused_computation.7.clone.1 | convolution fusion | flops 411303936 | bytes 9789952 | tf_op jit(solution)/shard_map/while/body/eval_jaxpr/jtqk,kjd->jtqd/dot_general | solution.py:72
  269.1 1.5 fusion.51
  272.0 4.4 %bitcast_add_fusion.6 = f32[1,384,8,128]{3,1,2,0:T(8,128)} fusion(f32[1,384,8,128]{3,1,2,0:T(8,128)} %get-tuple-element.220, f32[512,384,8]{1,0,2:T(8,128)S(1)} %get-tuple-element.204, f32[384,8]{0,1:T(8,128)S(1)} %bitcast.122, pred[384,512]{0,1:T(8,128)(4,1)S(1)} %compare_and_fusion.4, f32[384,8]{0,1:T(8,128)S(1)} %get-tuple-element.205, ...), kind=kOutput, calls=%fused_computation.7.clone.1 | convolution fusion | flops 411303936 | bytes 9789952 | tf_op jit(solution)/shard_map/while/body/eval_jaxpr/jtqk,kjd->jtqd/dot_general | solution.py:72
  276.4 1.5 fusion.51
  279.3 4.4 %bitcast_add_fusion.6 = f32[1,384,8,128]{3,1,2,0:T(8,128)} fusion(f32[1,384,8,128]{3,1,2,0:T(8,128)} %get-tuple-element.220, f32[512,384,8]{1,0,2:T(8,128)S(1)} %get-tuple-element.204, f32[384,8]{0,1:T(8,128)S(1)} %bitcast.122, pred[384,512]{0,1:T(8,128)(4,1)S(1)} %compare_and_fusion.4, f32[384,8]{0,1:T(8,128)S(1)} %get-tuple-element.205, ...), kind=kOutput, calls=%fused_computation.7.clone.1 | convolution fusion | flops 411303936 | bytes 9789952 | tf_op jit(solution)/shard_map/while/body/eval_jaxpr/jtqk,kjd->jtqd/dot_general | solution.py:72
  283.7 1.5 fusion.51
  286.6 4.4 %bitcast_add_fusion.6 = f32[1,384,8,128]{3,1,2,0:T(8,128)} fusion(f32[1,384,8,128]{3,1,2,0:T(8,128)} %get-tuple-element.220, f32[512,384,8]{1,0,2:T(8,128)S(1)} %get-tuple-element.204, f32[384,8]{0,1:T(8,128)S(1)} %bitcast.122, pred[384,512]{0,1:T(8,128)(4,1)S(1)} %compare_and_fusion.4, f32[384,8]{0,1:T(8,128)S(1)} %get-tuple-element.205, ...), kind=kOutput, calls=%fused_computation.7.clone.1 | convolution fusion | flops 411303936 | bytes 9789952 | tf_op jit(solution)/shard_map/while/body/eval_jaxpr/jtqk,kjd->jtqd/dot_general | solution.py:72
  290.9 1.5 fusion.51
  293.9 4.4 %bitcast_add_fusion.6 = f32[1,384,8,128]{3,1,2,0:T(8,128)} fusion(f32[1,384,8,128]{3,1,2,0:T(8,128)} %get-tuple-element.220, f32[512,384,8]{1,0,2:T(8,128)S(1)} %get-tuple-element.204, f32[384,8]{0,1:T(8,128)S(1)} %bitcast.122, pred[384,512]{0,1:T(8,128)(4,1)S(1)} %compare_and_fusion.4, f32[384,8]{0,1:T(8,128)S(1)} %get-tuple-element.205, ...), kind=kOutput, calls=%fused_computation.7.clone.1 | convolution fusion | flops 411303936 | bytes 9789952 | tf_op jit(solution)/shard_map/while/body/eval_jaxpr/jtqk,kjd->jtqd/dot_general | solution.py:72
  298.2 1.5 fusion.51
  301.1 4.4 %bitcast_add_fusion.6 = f32[1,384,8,128]{3,1,2,0:T(8,128)} fusion(f32[1,384,8,128]{3,1,2,0:T(8,128)} %get-tuple-element.220, f32[512,384,8]{1,0,2:T(8,128)S(1)} %get-tuple-element.204, f32[384,8]{0,1:T(8,128)S(1)} %bitcast.122, pred[384,512]{0,1:T(8,128)(4,1)S(1)} %compare_and_fusion.4, f32[384,8]{0,1:T(8,128)S(1)} %get-tuple-element.205, ...), kind=kOutput, calls=%fused_computation.7.clone.1 | convolution fusion | flops 411303936 | bytes 9789952 | tf_op jit(solution)/shard_map/while/body/eval_jaxpr/jtqk,kjd->jtqd/dot_general | solution.py:72
  305.5 1.5 fusion.51
  308.4 4.4 %bitcast_add_fusion.6 = f32[1,384,8,128]{3,1,2,0:T(8,128)} fusion(f32[1,384,8,128]{3,1,2,0:T(8,128)} %get-tuple-element.220, f32[512,384,8]{1,0,2:T(8,128)S(1)} %get-tuple-element.204, f32[384,8]{0,1:T(8,128)S(1)} %bitcast.122, pred[384,512]{0,1:T(8,128)(4,1)S(1)} %compare_and_fusion.4, f32[384,8]{0,1:T(8,128)S(1)} %get-tuple-element.205, ...), kind=kOutput, calls=%fused_computation.7.clone.1 | convolution fusion | flops 411303936 | bytes 9789952 | tf_op jit(solution)/shard_map/while/body/eval_jaxpr/jtqk,kjd->jtqd/dot_general | solution.py:72
  312.8 1.5 fusion.51
  315.7 4.4 %bitcast_add_fusion.6 = f32[1,384,8,128]{3,1,2,0:T(8,128)} fusion(f32[1,384,8,128]{3,1,2,0:T(8,128)} %get-tuple-element.220, f32[512,384,8]{1,0,2:T(8,128)S(1)} %get-tuple-element.204, f32[384,8]{0,1:T(8,128)S(1)} %bitcast.122, pred[384,512]{0,1:T(8,128)(4,1)S(1)} %compare_and_fusion.4, f32[384,8]{0,1:T(8,128)S(1)} %get-tuple-element.205, ...), kind=kOutput, calls=%fused_computation.7.clone.1 | convolution fusion | flops 411303936 | bytes 9789952 | tf_op jit(solution)/shard_map/while/body/eval_jaxpr/jtqk,kjd->jtqd/dot_general | solution.py:72
  320.1 1.5 fusion.51
  323.0 4.4 %bitcast_add_fusion.6 = f32[1,384,8,128]{3,1,2,0:T(8,128)} fusion(f32[1,384,8,128]{3,1,2,0:T(8,128)} %get-tuple-element.220, f32[512,384,8]{1,0,2:T(8,128)S(1)} %get-tuple-element.204, f32[384,8]{0,1:T(8,128)S(1)} %bitcast.122, pred[384,512]{0,1:T(8,128)(4,1)S(1)} %compare_and_fusion.4, f32[384,8]{0,1:T(8,128)S(1)} %get-tuple-element.205, ...), kind=kOutput, calls=%fused_computation.7.clone.1 | convolution fusion | flops 411303936 | bytes 9789952 | tf_op jit(solution)/shard_map/while/body/eval_jaxpr/jtqk,kjd->jtqd/dot_general | solution.py:72
  327.4 1.5 fusion.51
  330.3 4.4 %bitcast_add_fusion.6 = f32[1,384,8,128]{3,1,2,0:T(8,128)} fusion(f32[1,384,8,128]{3,1,2,0:T(8,128)} %get-tuple-element.220, f32[512,384,8]{1,0,2:T(8,128)S(1)} %get-tuple-element.204, f32[384,8]{0,1:T(8,128)S(1)} %bitcast.122, pred[384,512]{0,1:T(8,128)(4,1)S(1)} %compare_and_fusion.4, f32[384,8]{0,1:T(8,128)S(1)} %get-tuple-element.205, ...), kind=kOutput, calls=%fused_computation.7.clone.1 | convolution fusion | flops 411303936 | bytes 9789952 | tf_op jit(solution)/shard_map/while/body/eval_jaxpr/jtqk,kjd->jtqd/dot_general | solution.py:72
  334.6 1.5 fusion.51
  336.2 1.9 select_convert_fusion
  (129 shorter events, 27.5 us)
Async XLA Ops:
  6.5 73.4 %all-gather.2.cloned.1.call-start = ((), (), s32[]{:S(2)}) async-start(), calls=%async_computation.1 | async-start | bytes 4325376 | tf_op jit(solution)/shard_map/all_gather | solution.py:101
  7.3 121.8 %collective-permute-start = (bf16[2,384,128]{2,1,0:T(8,128)(2,1)}, bf16[2,384,128]{2,1,0:T(8,128)(2,1)S(1)}, u32[]{:S(2)}, u32[]{:S(2)}) collective-permute-start(bf16[2,384,128]{2,1,0:T(8,128)(2,1)} %param.10), channel_id=1, source_target_pairs={{0,8},{8,16},{16,24},{24,32},{32,40},{40,48},{48,56},{56,64},{64,7... | collective-permute-start | bytes 589832 | tf_op jit(solution)/shard_map/ppermute | solution.py:17
  121.8 7.3 %copy-start.1 = (bf16[2,384,128]{2,1,0:T(8,128)(2,1)S(1)}, bf16[2,384,128]{2,1,0:T(8,128)(2,1)}, u32[]{:S(2)}) copy-start(bf16[2,384,128]{2,1,0:T(8,128)(2,1)} %param.10) | copy-start | bytes 589828
  121.8 7.3 %copy-start = (bf16[384,1024]{1,0:T(8,128)(2,1)S(1)}, bf16[384,1024]{1,0:T(8,128)(2,1)}, u32[]{:S(2)}) copy-start(bf16[384,1024]{1,0:T(8,128)(2,1)} %param.9) | copy-start | bytes 2359300
  121.8 55.0 %all-to-all-start = ((bf16[8,2,131072]{2,1,0:T(2,128)(2,1)}), bf16[8,2,131072]{2,1,0:T(2,128)(2,1)}, u32[]{:S(2)}, u32[]{:S(2)}) async-start(bf16[8,2,131072]{2,1,0:T(2,128)(2,1)} %reshape.344), calls=%async_computation | async-start | bytes 8388608 | tf_op jit(solution)/shard_map/all_to_all | solution.py:102
Sparse Core Ops, SparseCore 0:
  9.2 70.6 all-gather.1
where the time goes:
time: 348 us; the launch traced here: 347 us
  waiting for transfers between devices  105 us (30%)
  matrix products  93.4 us (27%)
  local copies, waits for them, and re-layouts  88.6 us (25%)
  other arithmetic  34.7 us (10%)
  between operations  13.6 us (4%)
  starting transfers between devices  10.8 us (3%)
    dot_general x17, matrix products, absorb(): jnp.einsum('jtqk,kjd->jtqd', weights.astype(jnp.bfloat16), value_rows, pr...  73.8 us
    all_gather x1, waiting for transfers between devices, per_device(): stored = lax.all_gather(prefix_kv, 'req', axis=1, tiled=True)  64.1 us
    all_to_all x1, waiting for transfers between devices, per_device(): lax.all_to_all(stored, 'tp', split_axis=3, concat_axis=2, tiled=True)  39.8 us
    unnamed x10, local copies, waits for them, and re-layouts  33.7 us
    reduce_sum x17, other arithmetic, absorb(): new_sum = running_sum * shrink + jnp.sum(weights, axis=-1)  26.4 us
    all_gather x1, local copies, waits for them, and re-layouts, per_device(): stored = lax.all_gather(prefix_kv, 'req', axis=1, tiled=True)  23.2 us
    slice x2, local copies, waits for them, and re-layouts, per_device(): value_rows = relaid[1].reshape(passes, stride * block_rows, kv_heads, HD)  21.9 us
    dot_general x17, matrix products, absorb(): jnp.einsum('tjqd,kjd->jtqk', query_heads, key_rows, preferred_element_typ...  19.6 us
  transfers between devices with their start and end apart: 3, of which 2 were waited for; matrix products, arithmetic and copies ran while one was open for 16% of the time, Pallas kernels for 0%

commit v1 on v0

--- a/solution.py
+++ b/solution.py
@@ -98,7 +98,15 @@
         nearby[1].reshape(2 * tok_rows, kv_heads, HD),
         near_allowed,
     )
-    stored = lax.all_gather(prefix_kv, "req", axis=1, tiled=True)
+    stored = jnp.concatenate(
+        lax.all_to_all(
+            jnp.stack(lax.axis_size("req") * [prefix_kv]),
+            axis_name="req",
+            split_axis=0,
+            concat_axis=0,
+        ),
+        1,
+    )
     relaid = lax.all_to_all(stored, "tp", split_axis=3, concat_axis=2, tiled=True)
     status = carried
     extent = relaid.shape[1]

time: 348 us -> 361 us (1.037)
  waiting for transfers between devices: 105 us -> 129 us
  between operations: 13.6 us -> 0.28 us
  starting transfers between devices: 10.8 us -> 21.1 us
  local copies, waits for them, and re-layouts: 88.6 us -> 80.6 us
    all_to_all x0 -> x1, waiting for transfers between devices: none -> 88.9 us  [per_device(): lax.all_to_all(jnp.stack(lax.axis_size('req') * [prefix_kv]), axis_name='...]
    all_gather x1 -> x0, waiting for transfers between devices: 64.1 us -> none  [per_device(): stored = lax.all_gather(prefix_kv, 'req', axis=1, tiled=True)]
    reshape x0 -> x1, local copies, waits for them, and re-layouts: none -> 23.2 us  [per_device(): jnp.concatenate(lax.all_to_all(jnp.stack(lax.axis_size('req') * [prefix_k...]
    all_gather x1 -> x0, local copies, waits for them, and re-layouts: 23.2 us -> none  [per_device(): stored = lax.all_gather(prefix_kv, 'req', axis=1, tiled=True)]
    slice x2, local copies, waits for them, and re-layouts: 21.9 us -> 4.54 us  [per_device(): value_rows = relaid[1].reshape(passes, stride * block_rows, kv_heads, HD)]
    all_to_all x0 -> x1, local copies, waits for them, and re-layouts: none -> 15 us  [per_device(): lax.all_to_all(stored, 'tp', split_axis=3, concat_axis=2, tiled=True)]
    all_to_all x0 -> x1, starting transfers between devices: none -> 11.2 us  [per_device(): lax.all_to_all(jnp.stack(lax.axis_size('req') * [prefix_kv]), axis_name='...]
    slice x1, local copies, waits for them, and re-layouts: 8.46 us -> 0.48 us  [per_device(): key_rows = relaid[0].reshape(passes, stride * block_rows, kv_heads, HD)]
  transfers between devices with their start and end apart: 3 -> 3, of which waited for: 2 -> 2; matrix products, arithmetic and copies ran while one was open for 16% -> 15% of each run, Pallas kernels for 0% -> 0%
where the time goes in v1:
time: 361 us; the launch traced here: 358 us
  waiting for transfers between devices  129 us (36%)
  matrix products  93.1 us (26%)
  local copies, waits for them, and re-layouts  80.6 us (22%)
  other arithmetic  33.4 us (9%)
  starting transfers between devices  21.1 us (6%)
    all_to_all x1, waiting for transfers between devices, per_device(): lax.all_to_all(jnp.stack(lax.axis_size('req') * [prefix_kv]), axis_name='...  88.9 us
    dot_general x17, matrix products, absorb(): jnp.einsum('jtqk,kjd->jtqd', weights.astype(jnp.bfloat16), value_rows, pr...  73.5 us
    all_to_all x1, waiting for transfers between devices, per_device(): lax.all_to_all(stored, 'tp', split_axis=3, concat_axis=2, tiled=True)  39.8 us
    unnamed x18, local copies, waits for them, and re-layouts  32.6 us
    reduce_sum x17, other arithmetic, absorb(): new_sum = running_sum * shrink + jnp.sum(weights, axis=-1)  26.4 us
    reshape x1, local copies, waits for them, and re-layouts, per_device(): jnp.concatenate(lax.all_to_all(jnp.stack(lax.axis_size('req') * [prefix_k...  23.2 us
    dot_general x17, matrix products, absorb(): jnp.einsum('tjqd,kjd->jtqk', query_heads, key_rows, preferred_element_typ...  19.6 us
    all_to_all x1, local copies, waits for them, and re-layouts, per_device(): lax.all_to_all(stored, 'tp', split_axis=3, concat_axis=2, tiled=True)  15 us
  transfers between devices with their start and end apart: 3, of which 2 were waited for; matrix products, arithmetic and copies ran while one was open for 15% of the time, Pallas kernels for 0%

profile of v1, /device:TPU:1, one launch (start us, length us, event | category | flops | bytes accessed | tf_op | source)
XLA Modules:
  0.0 358.2 jit_solution(14062530535330527204)
XLA Ops:
  0.0 3.4 stack.2
  3.5 11.2 %all-to-all-start = ((bf16[32,2,1,32,1024]{4,3,1,2,0:T(8,128)(2,1)}), bf16[32,2,1,32,1024]{4,3,1,2,0:T(8,128)(2,1)}, u32[]{:S(2)}, u32[]{:S(2)}) async-start(bf16[32,2,1,32,1024]{4,3,1,2,0:T(8,128)(2,1)} %stack.2), calls=%async_computation | async-start | bytes 8388608 | tf_op jit(solution)/shard_map/all_to_all | solution.py:102
  14.7 3.5 collective-permute-start
  19.9 88.9 %all-to-all-done = bf16[32,2,1,32,1024]{4,3,1,2,0:T(8,128)(2,1)} async-done(((bf16[32,2,1,32,1024]{4,3,1,2,0:T(8,128)(2,1)}), bf16[32,2,1,32,1024]{4,3,1,2,0:T(8,128)(2,1)}, u32[]{:S(2)}, u32[]{:S(2)}) %all-to-all-start) | async-done | bytes 4194336 | tf_op jit(solution)/shard_map/all_to_all | solution.py:102
  108.8 23.2 %copy.43 = bf16[2,32,32,1024]{2,1,0,3:T(8,128)(2,1)} copy(bf16[2,32,32,1024]{3,2,0,1:T(8,128)(2,1)} %bitcast.22) | data formatting | bytes 8388608 | tf_op jit(solution)/shard_map/reshape | solution.py:101
  131.9 18.7 %reshape.355 = bf16[8,2,131072]{2,1,0:T(2,128)(2,1)} reshape(bf16[1024,2,32,32]{3,2,1,0:T(8,128)(2,1)} %bitcast.126) | data formatting | bytes 8388608
  150.7 6.4 %all-to-all-start.1 = ((bf16[8,2,131072]{2,1,0:T(2,128)(2,1)}), bf16[8,2,131072]{2,1,0:T(2,128)(2,1)}, u32[]{:S(2)}, u32[]{:S(2)}) async-start(bf16[8,2,131072]{2,1,0:T(2,128)(2,1)} %reshape.355), calls=%async_computation.1 | async-start | bytes 8388608 | tf_op jit(solution)/shard_map/all_to_all | solution.py:110
  158.1 1.6 fusion.20
  159.8 2.2 fusion.22
  162.0 4.0 %add_bitcast_fusion = f32[1,384,8,128]{3,1,2,0:T(8,128)} fusion(f32[768,384,8]{1,0,2:T(8,128)S(1)} %get-tuple-element.136, f32[384,8]{0,1:T(8,128)S(1)} %get-tuple-element.134, pred[384,768]{0,1:T(8,128)(4,1)S(1)} %and_and_fusion, f32[384,8]{0,1:T(8,128)S(1)} %get-tuple-element.132, bf16[2,768,128]{2,1,0:T(8,128)(2,1)S(1)} %constant_dynamic-update-slice_fusion), kind=kOutput, calls=%fused_computation.33 | convolution fusion | flops 616169472 | bytes 11526144 | tf_op jit(solution)/shard_map/jtqk,kjd->jtqd/dot_general | solution.py:72
  166.0 39.8 %all-to-all-done.1 = bf16[8,2,131072]{2,1,0:T(2,128)(2,1)} async-done(((bf16[8,2,131072]{2,1,0:T(2,128)(2,1)}), bf16[8,2,131072]{2,1,0:T(2,128)(2,1)}, u32[]{:S(2)}, u32[]{:S(2)}) %all-to-all-start.1) | async-done | bytes 4194336 | tf_op jit(solution)/shard_map/all_to_all | solution.py:110
  205.8 12.4 %reshape.356 = bf16[1024,2,32,32]{3,2,1,0:T(8,128)(2,1)} reshape(bf16[8,2,131072]{2,1,0:T(2,128)(2,1)} %all-to-all-done.1) | data formatting | bytes 8388608
  218.2 15.0 %copy.54 = bf16[2,32,32,8,128]{4,3,2,1,0:T(8,128)(2,1)} copy(bf16[2,32,32,8,128]{2,1,0,4,3:T(8,128)(2,1)} %bitcast.127) | data formatting | bytes 8388608 | tf_op jit(solution)/shard_map/all_to_all | solution.py:110
  233.3 2.7 fusion.40
  236.5 1.8 copy.47
  238.3 116.3 %while.14 = (s32[]{:T(128)}, f32[1,384,8]{1,2,0:T(8,128)S(1)}, f32[1,384,8]{1,2,0:T(8,128)S(1)}, f32[1,384,8,128]{3,1,2,0:T(8,128)}, s32[16,512]{1,0:T(8,128)S(1...) while((s32[]{:T(128)}, f32[1,384,8]{1,2,0:T(8,128)S(1)}, ...), condition=%wide.region_13.14_spmd, body=%wide.region_10.13_spmd.sunk | while | flops 826942464 | bytes 24060404 | solution.py:126
  239.7 4.3 %bitcast_add_fusion.6 = f32[1,384,8,128]{3,1,2,0:T(8,128)} fusion(f32[1,384,8,128]{3,1,2,0:T(8,128)} %get-tuple-element.220, f32[512,384,8]{1,0,2:T(8,128)S(1)} %get-tuple-element.204, f32[384,8]{0,1:T(8,128)S(1)} %bitcast.129, pred[384,512]{0,1:T(8,128)(4,1)S(1)} %compare_and_fusion.4, f32[384,8]{0,1:T(8,128)S(1)} %get-tuple-element.205, ...), kind=kOutput, calls=%fused_computation.7.clone.1 | convolution fusion | flops 411303936 | bytes 9789952 | tf_op jit(solution)/shard_map/while/body/eval_jaxpr/jtqk,kjd->jtqd/dot_general | solution.py:72
  244.0 1.5 fusion.51
  246.9 4.3 %bitcast_add_fusion.6 = f32[1,384,8,128]{3,1,2,0:T(8,128)} fusion(f32[1,384,8,128]{3,1,2,0:T(8,128)} %get-tuple-element.220, f32[512,384,8]{1,0,2:T(8,128)S(1)} %get-tuple-element.204, f32[384,8]{0,1:T(8,128)S(1)} %bitcast.129, pred[384,512]{0,1:T(8,128)(4,1)S(1)} %compare_and_fusion.4, f32[384,8]{0,1:T(8,128)S(1)} %get-tuple-element.205, ...), kind=kOutput, calls=%fused_computation.7.clone.1 | convolution fusion | flops 411303936 | bytes 9789952 | tf_op jit(solution)/shard_map/while/body/eval_jaxpr/jtqk,kjd->jtqd/dot_general | solution.py:72
  251.3 1.5 fusion.51
  254.2 4.3 %bitcast_add_fusion.6 = f32[1,384,8,128]{3,1,2,0:T(8,128)} fusion(f32[1,384,8,128]{3,1,2,0:T(8,128)} %get-tuple-element.220, f32[512,384,8]{1,0,2:T(8,128)S(1)} %get-tuple-element.204, f32[384,8]{0,1:T(8,128)S(1)} %bitcast.129, pred[384,512]{0,1:T(8,128)(4,1)S(1)} %compare_and_fusion.4, f32[384,8]{0,1:T(8,128)S(1)} %get-tuple-element.205, ...), kind=kOutput, calls=%fused_computation.7.clone.1 | convolution fusion | flops 411303936 | bytes 9789952 | tf_op jit(solution)/shard_map/while/body/eval_jaxpr/jtqk,kjd->jtqd/dot_general | solution.py:72
  258.6 1.5 fusion.51
  261.5 4.3 %bitcast_add_fusion.6 = f32[1,384,8,128]{3,1,2,0:T(8,128)} fusion(f32[1,384,8,128]{3,1,2,0:T(8,128)} %get-tuple-element.220, f32[512,384,8]{1,0,2:T(8,128)S(1)} %get-tuple-element.204, f32[384,8]{0,1:T(8,128)S(1)} %bitcast.129, pred[384,512]{0,1:T(8,128)(4,1)S(1)} %compare_and_fusion.4, f32[384,8]{0,1:T(8,128)S(1)} %get-tuple-element.205, ...), kind=kOutput, calls=%fused_computation.7.clone.1 | convolution fusion | flops 411303936 | bytes 9789952 | tf_op jit(solution)/shard_map/while/body/eval_jaxpr/jtqk,kjd->jtqd/dot_general | solution.py:72
  265.8 1.5 fusion.51
  268.7 4.3 %bitcast_add_fusion.6 = f32[1,384,8,128]{3,1,2,0:T(8,128)} fusion(f32[1,384,8,128]{3,1,2,0:T(8,128)} %get-tuple-element.220, f32[512,384,8]{1,0,2:T(8,128)S(1)} %get-tuple-element.204, f32[384,8]{0,1:T(8,128)S(1)} %bitcast.129, pred[384,512]{0,1:T(8,128)(4,1)S(1)} %compare_and_fusion.4, f32[384,8]{0,1:T(8,128)S(1)} %get-tuple-element.205, ...), kind=kOutput, calls=%fused_computation.7.clone.1 | convolution fusion | flops 411303936 | bytes 9789952 | tf_op jit(solution)/shard_map/while/body/eval_jaxpr/jtqk,kjd->jtqd/dot_general | solution.py:72
  273.1 1.5 fusion.51
  276.0 4.3 %bitcast_add_fusion.6 = f32[1,384,8,128]{3,1,2,0:T(8,128)} fusion(f32[1,384,8,128]{3,1,2,0:T(8,128)} %get-tuple-element.220, f32[512,384,8]{1,0,2:T(8,128)S(1)} %get-tuple-element.204, f32[384,8]{0,1:T(8,128)S(1)} %bitcast.129, pred[384,512]{0,1:T(8,128)(4,1)S(1)} %compare_and_fusion.4, f32[384,8]{0,1:T(8,128)S(1)} %get-tuple-element.205, ...), kind=kOutput, calls=%fused_computation.7.clone.1 | convolution fusion | flops 411303936 | bytes 9789952 | tf_op jit(solution)/shard_map/while/body/eval_jaxpr/jtqk,kjd->jtqd/dot_general | solution.py:72
  280.4 1.5 fusion.51
  283.3 4.3 %bitcast_add_fusion.6 = f32[1,384,8,128]{3,1,2,0:T(8,128)} fusion(f32[1,384,8,128]{3,1,2,0:T(8,128)} %get-tuple-element.220, f32[512,384,8]{1,0,2:T(8,128)S(1)} %get-tuple-element.204, f32[384,8]{0,1:T(8,128)S(1)} %bitcast.129, pred[384,512]{0,1:T(8,128)(4,1)S(1)} %compare_and_fusion.4, f32[384,8]{0,1:T(8,128)S(1)} %get-tuple-element.205, ...), kind=kOutput, calls=%fused_computation.7.clone.1 | convolution fusion | flops 411303936 | bytes 9789952 | tf_op jit(solution)/shard_map/while/body/eval_jaxpr/jtqk,kjd->jtqd/dot_general | solution.py:72
  287.6 1.5 fusion.51
  290.6 4.3 %bitcast_add_fusion.6 = f32[1,384,8,128]{3,1,2,0:T(8,128)} fusion(f32[1,384,8,128]{3,1,2,0:T(8,128)} %get-tuple-element.220, f32[512,384,8]{1,0,2:T(8,128)S(1)} %get-tuple-element.204, f32[384,8]{0,1:T(8,128)S(1)} %bitcast.129, pred[384,512]{0,1:T(8,128)(4,1)S(1)} %compare_and_fusion.4, f32[384,8]{0,1:T(8,128)S(1)} %get-tuple-element.205, ...), kind=kOutput, calls=%fused_computation.7.clone.1 | convolution fusion | flops 411303936 | bytes 9789952 | tf_op jit(solution)/shard_map/while/body/eval_jaxpr/jtqk,kjd->jtqd/dot_general | solution.py:72
  294.9 1.5 fusion.51
  297.8 4.3 %bitcast_add_fusion.6 = f32[1,384,8,128]{3,1,2,0:T(8,128)} fusion(f32[1,384,8,128]{3,1,2,0:T(8,128)} %get-tuple-element.220, f32[512,384,8]{1,0,2:T(8,128)S(1)} %get-tuple-element.204, f32[384,8]{0,1:T(8,128)S(1)} %bitcast.129, pred[384,512]{0,1:T(8,128)(4,1)S(1)} %compare_and_fusion.4, f32[384,8]{0,1:T(8,128)S(1)} %get-tuple-element.205, ...), kind=kOutput, calls=%fused_computation.7.clone.1 | convolution fusion | flops 411303936 | bytes 9789952 | tf_op jit(solution)/shard_map/while/body/eval_jaxpr/jtqk,kjd->jtqd/dot_general | solution.py:72
  302.2 1.5 fusion.51
  305.1 4.3 %bitcast_add_fusion.6 = f32[1,384,8,128]{3,1,2,0:T(8,128)} fusion(f32[1,384,8,128]{3,1,2,0:T(8,128)} %get-tuple-element.220, f32[512,384,8]{1,0,2:T(8,128)S(1)} %get-tuple-element.204, f32[384,8]{0,1:T(8,128)S(1)} %bitcast.129, pred[384,512]{0,1:T(8,128)(4,1)S(1)} %compare_and_fusion.4, f32[384,8]{0,1:T(8,128)S(1)} %get-tuple-element.205, ...), kind=kOutput, calls=%fused_computation.7.clone.1 | convolution fusion | flops 411303936 | bytes 9789952 | tf_op jit(solution)/shard_map/while/body/eval_jaxpr/jtqk,kjd->jtqd/dot_general | solution.py:72
  309.5 1.5 fusion.51
  312.4 4.3 %bitcast_add_fusion.6 = f32[1,384,8,128]{3,1,2,0:T(8,128)} fusion(f32[1,384,8,128]{3,1,2,0:T(8,128)} %get-tuple-element.220, f32[512,384,8]{1,0,2:T(8,128)S(1)} %get-tuple-element.204, f32[384,8]{0,1:T(8,128)S(1)} %bitcast.129, pred[384,512]{0,1:T(8,128)(4,1)S(1)} %compare_and_fusion.4, f32[384,8]{0,1:T(8,128)S(1)} %get-tuple-element.205, ...), kind=kOutput, calls=%fused_computation.7.clone.1 | convolution fusion | flops 411303936 | bytes 9789952 | tf_op jit(solution)/shard_map/while/body/eval_jaxpr/jtqk,kjd->jtqd/dot_general | solution.py:72
  316.7 1.5 fusion.51
  319.6 4.3 %bitcast_add_fusion.6 = f32[1,384,8,128]{3,1,2,0:T(8,128)} fusion(f32[1,384,8,128]{3,1,2,0:T(8,128)} %get-tuple-element.220, f32[512,384,8]{1,0,2:T(8,128)S(1)} %get-tuple-element.204, f32[384,8]{0,1:T(8,128)S(1)} %bitcast.129, pred[384,512]{0,1:T(8,128)(4,1)S(1)} %compare_and_fusion.4, f32[384,8]{0,1:T(8,128)S(1)} %get-tuple-element.205, ...), kind=kOutput, calls=%fused_computation.7.clone.1 | convolution fusion | flops 411303936 | bytes 9789952 | tf_op jit(solution)/shard_map/while/body/eval_jaxpr/jtqk,kjd->jtqd/dot_general | solution.py:72
  324.0 1.5 fusion.51
  326.9 4.3 %bitcast_add_fusion.6 = f32[1,384,8,128]{3,1,2,0:T(8,128)} fusion(f32[1,384,8,128]{3,1,2,0:T(8,128)} %get-tuple-element.220, f32[512,384,8]{1,0,2:T(8,128)S(1)} %get-tuple-element.204, f32[384,8]{0,1:T(8,128)S(1)} %bitcast.129, pred[384,512]{0,1:T(8,128)(4,1)S(1)} %compare_and_fusion.4, f32[384,8]{0,1:T(8,128)S(1)} %get-tuple-element.205, ...), kind=kOutput, calls=%fused_computation.7.clone.1 | convolution fusion | flops 411303936 | bytes 9789952 | tf_op jit(solution)/shard_map/while/body/eval_jaxpr/jtqk,kjd->jtqd/dot_general | solution.py:72
  331.3 1.5 fusion.51
  334.2 4.3 %bitcast_add_fusion.6 = f32[1,384,8,128]{3,1,2,0:T(8,128)} fusion(f32[1,384,8,128]{3,1,2,0:T(8,128)} %get-tuple-element.220, f32[512,384,8]{1,0,2:T(8,128)S(1)} %get-tuple-element.204, f32[384,8]{0,1:T(8,128)S(1)} %bitcast.129, pred[384,512]{0,1:T(8,128)(4,1)S(1)} %compare_and_fusion.4, f32[384,8]{0,1:T(8,128)S(1)} %get-tuple-element.205, ...), kind=kOutput, calls=%fused_computation.7.clone.1 | convolution fusion | flops 411303936 | bytes 9789952 | tf_op jit(solution)/shard_map/while/body/eval_jaxpr/jtqk,kjd->jtqd/dot_general | solution.py:72
  338.5 1.5 fusion.51
  341.5 4.3 %bitcast_add_fusion.6 = f32[1,384,8,128]{3,1,2,0:T(8,128)} fusion(f32[1,384,8,128]{3,1,2,0:T(8,128)} %get-tuple-element.220, f32[512,384,8]{1,0,2:T(8,128)S(1)} %get-tuple-element.204, f32[384,8]{0,1:T(8,128)S(1)} %bitcast.129, pred[384,512]{0,1:T(8,128)(4,1)S(1)} %compare_and_fusion.4, f32[384,8]{0,1:T(8,128)S(1)} %get-tuple-element.205, ...), kind=kOutput, calls=%fused_computation.7.clone.1 | convolution fusion | flops 411303936 | bytes 9789952 | tf_op jit(solution)/shard_map/while/body/eval_jaxpr/jtqk,kjd->jtqd/dot_general | solution.py:72
  348.7 4.3 %bitcast_add_fusion.6 = f32[1,384,8,128]{3,1,2,0:T(8,128)} fusion(f32[1,384,8,128]{3,1,2,0:T(8,128)} %get-tuple-element.220, f32[512,384,8]{1,0,2:T(8,128)S(1)} %get-tuple-element.204, f32[384,8]{0,1:T(8,128)S(1)} %bitcast.129, pred[384,512]{0,1:T(8,128)(4,1)S(1)} %compare_and_fusion.4, f32[384,8]{0,1:T(8,128)S(1)} %get-tuple-element.205, ...), kind=kOutput, calls=%fused_computation.7.clone.1 | convolution fusion | flops 411303936 | bytes 9789952 | tf_op jit(solution)/shard_map/while/body/eval_jaxpr/jtqk,kjd->jtqd/dot_general | solution.py:72
  353.1 1.5 fusion.51
  354.6 1.9 select_convert_fusion
  (138 shorter events, 27.8 us)
Async XLA Ops:
  0.0 14.7 %copy-start.1 = (bf16[2,384,128]{2,1,0:T(8,128)(2,1)S(1)}, bf16[2,384,128]{2,1,0:T(8,128)(2,1)}, u32[]{:S(2)}) copy-start(bf16[2,384,128]{2,1,0:T(8,128)(2,1)} %param.10) | copy-start | bytes 589828
  0.0 18.3 %copy-start = (bf16[384,1024]{1,0:T(8,128)(2,1)S(1)}, bf16[384,1024]{1,0:T(8,128)(2,1)}, u32[]{:S(2)}) copy-start(bf16[384,1024]{1,0:T(8,128)(2,1)} %param.9) | copy-start | bytes 2359300
  3.4 15.6 %copy-start.5 = (s32[32]{0:T(128)S(1)}, s32[32]{0:T(128)}, u32[]{:S(2)}) copy-start(s32[32]{0:T(128)} %param.15) | copy-start | bytes 388
  3.5 15.9 %copy-start.2 = (s32[31]{0:T(128)S(1)}, s32[31]{0:T(128)}, u32[]{:S(2)}) copy-start(s32[31]{0:T(128)} %param.13) | copy-start | bytes 376
  3.5 15.9 %copy-start.3 = (s32[31]{0:T(128)S(1)}, s32[31]{0:T(128)}, u32[]{:S(2)}) copy-start(s32[31]{0:T(128)} %param.14) | copy-start | bytes 376
  3.5 16.0 %copy-start.4 = (s32[31]{0:T(128)S(1)}, s32[31]{0:T(128)}, u32[]{:S(2)}) copy-start(s32[31]{0:T(128)} %param.12) | copy-start | bytes 376
  3.5 105.3 %all-to-all-start = ((bf16[32,2,1,32,1024]{4,3,1,2,0:T(8,128)(2,1)}), bf16[32,2,1,32,1024]{4,3,1,2,0:T(8,128)(2,1)}, u32[]{:S(2)}, u32[]{:S(2)}) async-start(bf16[32,2,1,32,1024]{4,3,1,2,0:T(8,128)(2,1)} %stack.2), calls=%async_computation | async-start | bytes 8388608 | tf_op jit(solution)/shard_map/all_to_all | solution.py:102
  14.7 143.3 %collective-permute-start = (bf16[2,384,128]{2,1,0:T(8,128)(2,1)S(1)}, bf16[2,384,128]{2,1,0:T(8,128)(2,1)S(1)}, u32[]{:S(2)}, u32[]{:S(2)}) collective-permute-start(bf16[2,384,128]{2,1,0:T(8,128)(2,1)S(1)} %copy-done.1), channel_id=1, source_target_pairs={{0,8},{8,16},{16,24},{24,32},{32,40},{40,48},{48,56},{56,64},{64,7... | collective-permute-start | bytes 589832 | tf_op jit(solution)/shard_map/ppermute | solution.py:17
  150.7 55.1 %all-to-all-start.1 = ((bf16[8,2,131072]{2,1,0:T(2,128)(2,1)}), bf16[8,2,131072]{2,1,0:T(2,128)(2,1)}, u32[]{:S(2)}, u32[]{:S(2)}) async-start(bf16[8,2,131072]{2,1,0:T(2,128)(2,1)} %reshape.355), calls=%async_computation.1 | async-start | bytes 8388608 | tf_op jit(solution)/shard_map/all_to_all | solution.py:110
